TPU v7x, 512 devices: a whole 4x8x8 slice. The times are simulated.
512 devices in a mesh: shard: 128 (over y, z, core), tensor: 4 (over x).
Axes of the slice: x: 4, y: 8, z: 8, core: 2. Of those that a mesh axis runs over, the one named last changes fastest.
Arguments:
- big_grad: bfloat16 [32, 1280, 768], P(None, 'shard', 'tensor')
- big_weight: bfloat16 [32, 1280, 768], P(None, 'shard', 'tensor'), may hold values from -0.017944336 to 0.017944336
- big_moment: float32 [128, 768, 1280], P('shard', 'tensor'), may hold values from -6 to 6
- small_grad: bfloat16 [32, 1280, 192], P(None, 'shard')
- small_weight: bfloat16 [32, 1280, 192], P(None, 'shard'), may hold values from -0.15625 to 0.15625
- small_moment: float32 [128, 192, 1280], P('shard'), may hold values from -6 to 6
- owners: int32 [2, 32], replicated, may hold values from 0 to 127, as said below
- vec_parts: float32 [128, 43008], P('shard'), may hold values from -0.6 to 0.6
- vec_param: float32 [43008], P('shard'), may hold values from 0.5 to 1.5
- vec_first: float32 [43008], P('shard'), may hold values from -0.6 to 0.6
- vec_second: float32 [43008], P('shard'), may hold values from 0.01 to 1
Outputs:
- big_weight_new: bfloat16 [32, 1280, 768], P(None, 'shard', 'tensor')
- big_moment_new: float32 [128, 768, 1280], P('shard', 'tensor')
- small_weight_new: bfloat16 [32, 1280, 192], P(None, 'shard')
- small_moment_new: float32 [128, 192, 1280], P('shard')
- vec_param_new: float32 [43008], P('shard')
- vec_first_new: float32 [43008], P('shard')
- vec_second_new: float32 [43008], P('shard')
Inputs may be any that keep to these rules, and one draw needn't show every extreme that they name: `owners`: no shard index appears twice in the whole list (over both rows); each aligned group of four shard indices holds exactly one owner of each row; the first and the last shard index own a matrix.
All inputs are finite; a program needn't handle non-finite values.
Results may differ from a plain program's by a relative error of at most 0.0068.
Values may be sent and summed in bfloat16 or wider, within the bound.
No kernel may reach another device: no remote copies, remote signals or barrier semaphores. Data moves between devices by JAX's collectives and lax.ppermute only.
A program may use at most 64 MiB of HBM per device.

v0:
```python
import math
import jax
import jax.numpy as jnp
from jax import lax
from jax.sharding import PartitionSpec as P

D = 1280
ITERS = 2
newton_linear = 3.4445
newton_cubic = -4.775
newton_quintic = 2.0315
momentum_rate = 0.95
muon_rate = 0.05
weight_decay = 0.1
norm_epsilon = 1e-07
adam_rate = 0.004
first_decay = 0.9
second_decay = 0.95
adam_epsilon = 1e-08
first_correct = 0.99997343860111
second_correct = 0.99407947077967


def owner_table(owner_list, count):
    devices = lax.broadcasted_iota(jnp.int32, (count, owner_list.shape[0]), 0)
    return (devices == owner_list[None, :]).astype(jnp.bfloat16)


def route_rows(owner_map, pieces):
    flattened = pieces.reshape(pieces.shape[0], -1)
    routed = jnp.dot(owner_map, flattened, preferred_element_type=jnp.float32)
    return routed.astype(jnp.bfloat16).reshape((owner_map.shape[0],) + pieces.shape[1:])


def collect(owner_map, arrived):
    flattened = arrived.reshape(arrived.shape[0], -1)
    picked = lax.dot_general(
        owner_map, flattened, (((0,), (0,)), ((), ())), preferred_element_type=jnp.float32
    )
    return picked.astype(jnp.bfloat16).reshape((owner_map.shape[1],) + arrived.shape[1:])


def advance(arrived, moment, is_owner):
    gradient = arrived.T.astype(jnp.float32)
    renewed = momentum_rate * moment + gradient
    retained = jnp.where(is_owner, renewed, moment)
    blended = jnp.where(is_owner, gradient + momentum_rate * renewed, 0.0).astype(jnp.bfloat16).T
    return (retained, blended)


def normalized(field):
    values = field.astype(jnp.float32)
    squares = jnp.sum(values * values)
    return (values / (jnp.sqrt(squares) + norm_epsilon)).astype(jnp.bfloat16)


def gram_block(left_part, right_part):
    product = lax.dot_general(
        left_part, right_part, (((0,), (0,)), ((), ())), preferred_element_type=jnp.float32
    )
    return product.astype(jnp.bfloat16)


def poly_block(gram_part, gram_full):
    square = jnp.dot(gram_part, gram_full, preferred_element_type=jnp.float32)
    return (newton_cubic * gram_part.astype(jnp.float32) + newton_quintic * square).astype(
        jnp.bfloat16
    )


def newton_step(column_part, full_iterate, polynomial):
    product = lax.dot_general(
        full_iterate, polynomial, (((1,), (1,)), ((), ())), preferred_element_type=jnp.float32
    )
    return (newton_linear * column_part.astype(jnp.float32) + product).astype(jnp.bfloat16)


def small_newton(field):
    iterate = normalized(field)
    for iteration in range(ITERS):
        gram_full = gram_block(iterate, iterate)
        iterate = newton_step(iterate, iterate, poly_block(gram_full, gram_full))
    return iterate


def apply_update(weight, update):
    scale = 0.2 * math.sqrt(D)
    values = weight.astype(jnp.float32)
    return (
        values - muon_rate * (scale * update.astype(jnp.float32) + weight_decay * values)
    ).astype(jnp.bfloat16)


def gather_columns(column_part):
    return lax.all_gather(column_part, "tensor", axis=1, tiled=True)


def gather_gram(gram_part):
    return lax.all_gather(gram_part, "tensor", axis=0, tiled=True)


def per_device(
    big_grad,
    big_weight,
    big_moment,
    small_grad,
    small_weight,
    small_moment,
    owners,
    vec_parts,
    vec_param,
    vec_first,
    vec_second,
):
    shards = lax.axis_size("shard")
    shard_place = lax.axis_index("shard")
    column = lax.axis_index("tensor")
    block_width = big_grad.shape[2]
    rows_dev = big_grad.shape[1]
    matrices = big_grad.shape[0]
    joint_map = owner_table(jnp.concatenate([owners[0], owners[1]]), shards)
    joint_pieces = jnp.concatenate([big_grad, small_grad], axis=0)
    arrived = lax.all_to_all(
        route_rows(joint_map, joint_pieces), "shard", split_axis=0, concat_axis=1, tiled=True
    )[0]
    big_owner = jnp.any(owners[0] == shard_place)
    small_owner = jnp.any(owners[1] == shard_place)
    big_retained, big_blended = advance(arrived, big_moment[0], big_owner)
    small_retained, small_blended = advance(arrived, small_moment[0], small_owner)
    small_result = small_newton(small_blended)
    full_iterate = normalized(gather_columns(big_blended))
    for iteration in range(ITERS - 1):
        gram_full = gram_block(full_iterate, full_iterate)
        full_iterate = newton_step(full_iterate, full_iterate, poly_block(gram_full, gram_full))
    gram_full = gram_block(full_iterate, full_iterate)
    gram_rows = lax.dynamic_slice_in_dim(gram_full, column * block_width, block_width, 0)
    owned_part = lax.dynamic_slice_in_dim(full_iterate, column * block_width, block_width, 1)
    big_result = newton_step(owned_part, full_iterate, poly_block(gram_rows, gram_full))
    own_result = jnp.where(big_owner, big_result, small_result)
    returned = lax.all_to_all(
        own_result.reshape(shards, rows_dev, block_width),
        "shard",
        split_axis=0,
        concat_axis=0,
        tiled=True,
    )
    picked = collect(joint_map, returned)
    big_weight_new = apply_update(big_weight, picked[:matrices])
    small_weight_new = apply_update(small_weight, picked[matrices:])
    vec_pieces = vec_parts[0].reshape(shards, -1)
    grad_share = jnp.sum(
        lax.all_to_all(vec_pieces, "shard", split_axis=0, concat_axis=0, tiled=True), axis=0
    )
    first_new = first_decay * vec_first + (1.0 - first_decay) * grad_share
    second_new = second_decay * vec_second + (1.0 - second_decay) * grad_share * grad_share
    param_new = vec_param - adam_rate * (first_new / first_correct) / (
        jnp.sqrt(second_new / second_correct) + adam_epsilon
    )
    return (
        big_weight_new,
        big_retained[None],
        small_weight_new,
        small_retained[None],
        param_new,
        first_new,
        second_new,
    )


def solution(mesh):
    return jax.shard_map(
        per_device,
        mesh=mesh,
        in_specs=(
            P(None, "shard", "tensor"),
            P(None, "shard", "tensor"),
            P("shard", "tensor", None),
            P(None, "shard", None),
            P(None, "shard", None),
            P("shard", None, None),
            P(),
            P("shard", None),
            P("shard"),
            P("shard"),
            P("shard"),
        ),
        out_specs=(
            P(None, "shard", "tensor"),
            P("shard", "tensor", None),
            P(None, "shard", None),
            P("shard", None, None),
            P("shard"),
            P("shard"),
            P("shard"),
        ),
        check_vma=False,
    )
```

profile of v0, /device:TPU:1, one launch (start us, length us, event | category | flops | bytes accessed | tf_op | source)
XLA Modules:
  0.0 153.9 jit_solution(12986507688042528019)
XLA Ops:
  7.2 0.8 slice_bitcast_fusion.1
  7.9 1.0 pad_maximum_fusion
  9.0 0.2 copy.32
  9.2 0.4 reshape.45
  9.6 0.1 pad_add_fusion
  9.6 0.3 convolution_convert_fusion
  9.9 0.3 copy.33
  10.2 0.0 copy-start.5
  10.2 1.3 copy.34
  11.5 1.6 %reshape.59 = bf16[128,2,960]{2,1,0:T(2,128)(2,1)} reshape(bf16[128,10,192]{2,1,0:T(8,128)(2,1)S(1)} %copy.34) | data formatting | bytes 983040
  13.1 18.4 %all-to-all-start = ((bf16[128,2,960]{2,1,0:T(2,128)(2,1)}), bf16[128,2,960]{2,1,0:T(2,128)(2,1)S(1)}, u32[]{:S(2)}, u32[]{:S(2)}) async-start(bf16[128,2,960]{2,1,0:T(2,128)(2,1)} %reshape.59), calls=%async_computation | async-start | bytes 1048576 | tf_op jit(solution)/shard_map/all_to_all | solution.py:123
  31.5 0.0 all-gather.2.cloned.1.call-start
  31.6 0.0 copy-done.5
  31.6 0.6 compare_reduce_fusion.1
  32.2 18.7 %all-to-all-done = bf16[128,2,960]{2,1,0:T(2,128)(2,1)S(1)} async-done(((bf16[128,2,960]{2,1,0:T(2,128)(2,1)}), bf16[128,2,960]{2,1,0:T(2,128)(2,1)S(1)}, u32[]{:S(2)}, u32[]{:S(2)}) %all-to-all-start) | async-done | bytes 491552 | tf_op jit(solution)/shard_map/all_to_all | solution.py:123
  50.9 0.8 reshape.60
  51.7 0.4 reshape.49
  52.1 0.0 copy-start.1
  52.1 0.4 copy.35
  52.5 0.8 copy-done.1
  53.3 4.9 %fusion.17 = (f32[1,192,1280]{2,1,0:T(8,128)}, bf16[1280,192]{0,1:T(8,128)(2,1)}, f32[1,192,1280]{2,1,0:T(8,128)}, f32[]{:T(128)}, bf16[192,1280]{1,0:T(8,128)(2,1)S(1)}) fusion(f32[1,192,1280]{2,1,0:T(8,128)S(1)} %copy-done.1, f32[1280,192]{0,1:T(8,128)S(1)} %copy.35, pred[]{:T(512)} %get-tuple-element.21, f32[1,192,1280]{2,1,0:T(8,128)} %param.16, ...), kind=kLoop, calls=%fused_computation.39 | loop fusion | flops 4177919 | bytes 5898246 | tf_op jit(solution)/shard_map/broadcast_in_dim | solution.py:161
  58.2 0.0 all-gather.2.cloned.1.call-update
  58.2 0.5 broadcast.71
  58.7 0.0 copy-done.2
  58.7 1.0 reduce.5
  59.8 1.0 all_to_all.20
  60.8 7.3 %all-to-all-start.2 = ((f32[128,1,336]{2,1,0:T(1,128)}), f32[128,1,336]{2,1,0:T(1,128)S(1)}, u32[]{:S(2)}, u32[]{:S(2)}) async-start(f32[128,1,336]{2,1,0:T(1,128)} %all_to_all.20), calls=%async_computation.2 | async-start | bytes 393216 | tf_op jit(solution)/shard_map/all_to_all | solution.py:152
  68.7 0.3 convolution_convert_fusion.5
  69.1 0.4 fusion.3
  69.5 0.3 convolution_convert_fusion.4
  69.8 0.4 fusion.4
  70.3 16.5 %all-gather.2.cloned.1.call-done = bf16[1280,768]{0,1:T(8,128)(2,1)} async-done(((bf16[1280,192]{0,1:T(8,128)(2,1)}), bf16[1280,768]{0,1:T(8,128)(2,1)}) %all-gather.2.cloned.1.call-update) | async-done | bytes 1966096 | tf_op jit(solution)/shard_map/all_gather | solution.py:95
  86.8 3.3 %fusion = f32[]{:T(128)} fusion(bf16[1280,768]{0,1:T(8,128)(2,1)} %all-gather.2.cloned.1.call-done), kind=kLoop, calls=%fused_computation.2 | loop fusion | flops 2949119 | bytes 1966084 | tf_op jit(solution)/shard_map/reduce_sum | solution.py:53
  90.8 0.0 copy-done
  90.8 2.8 %convolution_convert_fusion.3 = bf16[768,768]{1,0:T(8,128)(2,1)} fusion(bf16[1280,768]{0,1:T(8,128)(2,1)S(1)} %copy-done, f32[]{:T(128)S(6)} %add.66), kind=kOutput, calls=%fused_computation.16 | convolution fusion | flops 1513488384 | bytes 3145732 | tf_op jit(solution)/shard_map/dot_general | solution.py:58
  93.6 6.3 %add_convert_fusion = bf16[1280,768]{0,1:T(8,128)(2,1)} fusion(bf16[768,768]{1,0:T(8,128)(2,1)} %convolution_convert_fusion.3, f32[]{:T(128)S(6)} %add.66, bf16[1280,768]{0,1:T(8,128)(2,1)S(1)} %copy-done), kind=kOutput, calls=%fused_computation.4 | convolution fusion | flops 2428698624 | bytes 5111812 | tf_op jit(solution)/shard_map/dot_general | solution.py:72
  99.9 3.8 %convolution_convert_fusion.2 = bf16[768,768]{1,0:T(8,128)(2,1)S(1)} fusion(bf16[1280,768]{0,1:T(8,128)(2,1)} %add_convert_fusion), kind=kOutput, calls=%fused_computation.15 | convolution fusion | flops 1510539264 | bytes 3145728 | tf_op jit(solution)/shard_map/dot_general | solution.py:58
  103.7 3.2 %fusion.5 = bf16[1280,192]{0,1:T(8,128)(2,1)S(1)} fusion(bf16[1280,192]{0,1:T(8,128)(2,1)S(1)} %fusion.4, bf16[1280,768]{0,1:T(8,128)(2,1)} %add_convert_fusion, bf16[768,768]{1,0:T(8,128)(2,1)S(1)} %convolution_convert_fusion.2, s32[]{:T(128)S(6)} %select_n.39, pred[]{:T(512)} %get-tuple-element.21), kind=kOutput, calls=%fused_computation.11 | convolution fusion | flops 605945856 | bytes 5212160 | tf_op jit(solution)/shard_map/dot_general | solution.py:72
  106.9 0.2 copy.36
  107.2 0.0 copy-start.6
  107.2 0.0 copy-start.7
  107.2 0.0 copy-start.8
  107.2 0.3 reshape.47
  107.5 1.6 %reshape.61 = bf16[128,2,960]{2,1,0:T(2,128)(2,1)} reshape(bf16[128,10,192]{2,1,0:T(8,128)(2,1)S(1)} %reshape.47) | data formatting | bytes 983040
  109.0 0.0 all-to-all-done.2
  109.1 14.5 %all-to-all-start.1 = ((bf16[128,2,960]{2,1,0:T(2,128)(2,1)}), bf16[128,2,960]{2,1,0:T(2,128)(2,1)S(1)}, u32[]{:S(2)}, u32[]{:S(2)}) async-start(bf16[128,2,960]{2,1,0:T(2,128)(2,1)} %reshape.61), calls=%async_computation.1 | async-start | bytes 1048576 | tf_op jit(solution)/shard_map/all_to_all | solution.py:140
  123.5 0.2 reduce_sum.29
  123.7 0.0 copy-done.6
  123.7 0.0 copy-done.7
  123.7 0.0 copy-done.8
  123.7 0.6 divide_subtract_fusion
  124.3 18.6 %all-to-all-done.1 = bf16[128,2,960]{2,1,0:T(2,128)(2,1)S(1)} async-done(((bf16[128,2,960]{2,1,0:T(2,128)(2,1)}), bf16[128,2,960]{2,1,0:T(2,128)(2,1)S(1)}, u32[]{:S(2)}, u32[]{:S(2)}) %all-to-all-start.1) | async-done | bytes 491552 | tf_op jit(solution)/shard_map/all_to_all | solution.py:140
  143.0 0.8 reshape.62
  143.7 0.0 copy-start.3
  143.7 0.7 copy.37
  144.5 0.3 convolution_convert_fusion.1
  144.8 0.0 copy-start.4
  144.9 0.2 mul.156
  145.0 0.0 copy-done.3
  145.0 0.2 fusion.26
  145.2 0.7 copy.40
  145.9 0.2 mul.160
  146.1 0.2 fusion.29
  146.3 0.7 copy.41
  (4 shorter events, 0.0 us)
Async XLA Ops:
  10.2 21.4 %copy-start.5 = (s32[2,32]{1,0:T(2,128)S(1)}, s32[2,32]{1,0:T(2,128)}, u32[]{:S(2)}) copy-start(s32[2,32]{1,0:T(2,128)} %param.17) | copy-start | bytes 772
  13.1 37.8 %all-to-all-start = ((bf16[128,2,960]{2,1,0:T(2,128)(2,1)}), bf16[128,2,960]{2,1,0:T(2,128)(2,1)S(1)}, u32[]{:S(2)}, u32[]{:S(2)}) async-start(bf16[128,2,960]{2,1,0:T(2,128)(2,1)} %reshape.59), calls=%async_computation | async-start | bytes 1048576 | tf_op jit(solution)/shard_map/all_to_all | solution.py:123
  31.5 55.3 %all-gather.2.cloned.1.call-start = ((), (), s32[]{:S(2)}) async-start(), calls=%async_computation.3 | async-start | bytes 2457600 | tf_op jit(solution)/shard_map/all_gather | solution.py:95
  52.1 1.2 copy-start.1
  53.3 5.4 %copy-start.2 = (f32[1,43008]{1,0:T(1,128)S(1)}, f32[1,43008]{1,0:T(1,128)}, u32[]{:S(2)}) copy-start(f32[1,43008]{1,0:T(1,128)} %param.18) | copy-start | bytes 516100
  60.8 48.3 %all-to-all-start.2 = ((f32[128,1,336]{2,1,0:T(1,128)}), f32[128,1,336]{2,1,0:T(1,128)S(1)}, u32[]{:S(2)}, u32[]{:S(2)}) async-start(f32[128,1,336]{2,1,0:T(1,128)} %all_to_all.20), calls=%async_computation.2 | async-start | bytes 393216 | tf_op jit(solution)/shard_map/all_to_all | solution.py:152
  86.8 4.0 %copy-start = (bf16[1280,768]{0,1:T(8,128)(2,1)S(1)}, bf16[1280,768]{0,1:T(8,128)(2,1)}, u32[]{:S(2)}) copy-start(bf16[1280,768]{0,1:T(8,128)(2,1)} %all-gather.2.cloned.1.call-done) | copy-start | bytes 5898244
  107.2 16.5 %copy-start.6 = (f32[336]{0:T(512)S(1)}, f32[336]{0:T(512)}, u32[]{:S(2)}) copy-start(f32[336]{0:T(512)} %param.19) | copy-start | bytes 4036
  107.2 16.5 %copy-start.7 = (f32[336]{0:T(512)S(1)}, f32[336]{0:T(512)}, u32[]{:S(2)}) copy-start(f32[336]{0:T(512)} %param.20) | copy-start | bytes 4036
  107.2 16.5 %copy-start.8 = (f32[336]{0:T(512)S(1)}, f32[336]{0:T(512)}, u32[]{:S(2)}) copy-start(f32[336]{0:T(512)} %param.21) | copy-start | bytes 4036
  109.1 33.9 %all-to-all-start.1 = ((bf16[128,2,960]{2,1,0:T(2,128)(2,1)}), bf16[128,2,960]{2,1,0:T(2,128)(2,1)S(1)}, u32[]{:S(2)}, u32[]{:S(2)}) async-start(bf16[128,2,960]{2,1,0:T(2,128)(2,1)} %reshape.61), calls=%async_computation.1 | async-start | bytes 1048576 | tf_op jit(solution)/shard_map/all_to_all | solution.py:140
  143.7 1.3 copy-start.3
  144.8 1.3 copy-start.4
Sparse Core Ops, SparseCore 0:
  58.3 28.4 all-gather.1
where the time goes:
time: 154 us
  waiting for transfers between devices  53.9 us (35%)
  starting transfers between devices  40.2 us (26%)
  matrix products  18.2 us (12%)
  between operations  15.7 us (10%)
  local copies, waits for them, and re-layouts  13.7 us (9%)
  other arithmetic  12.2 us (8%)
    all_to_all x1, waiting for transfers between devices, per_device(): lax.all_to_all(route_rows(joint_map, joint_pieces), 'shard', split_axis=0...  18.7 us
    all_to_all x1, waiting for transfers between devices, per_device(): lax.all_to_all(own_result.reshape(shards, rows_dev, block_width), 'shard'...  18.6 us
    all_to_all x1, starting transfers between devices, per_device(): lax.all_to_all(route_rows(joint_map, joint_pieces), 'shard', split_axis=0...  18.4 us
    all_gather x1, waiting for transfers between devices, gather_columns(): return lax.all_gather(column_part, 'tensor', axis=1, tiled=True)  16.5 us
    all_to_all x1, starting transfers between devices, per_device(): lax.all_to_all(own_result.reshape(shards, rows_dev, block_width), 'shard'...  14.5 us
    dot_general x4, matrix products, newton_step(): lax.dot_general(full_iterate, polynomial, (((1,), (1,)), ((), ())), prefe...  10.4 us
    unnamed x25, local copies, waits for them, and re-layouts  7.42 us
    all_to_all x1, starting transfers between devices, per_device(): lax.all_to_all(vec_pieces, 'shard', split_axis=0, concat_axis=0, tiled=True)  7.25 us
  transfers between devices with their start and end apart: 4, of which 3 were waited for; matrix products, arithmetic and copies ran while one was open for 17% of the time, Pallas kernels for 0%

commit v1 on v0

--- a/solution.py
+++ b/solution.py
@@ -1,3 +1,4 @@
+import functools
 import math
 import jax
 import jax.numpy as jnp
@@ -21,6 +22,19 @@
 second_correct = 0.99407947077967
 
 
+def map_floor_over_axis(u_in, a_name):
+    pieces_in = []
+    for _ in range(lax.axis_size(a_name)):
+        pieces_in.append(u_in)
+    block_now = jnp.stack(pieces_in, 0)
+    piece_now = lax.all_to_all(block_now, a_name, 0, 0)
+    y1 = jnp.concatenate(piece_now, axis=1)
+    return y1
+
+
+update_the_axis_part = functools.partial(map_floor_over_axis, a_name="tensor")
+
+
 def owner_table(owner_list, count):
     devices = lax.broadcasted_iota(jnp.int32, (count, owner_list.shape[0]), 0)
     return (devices == owner_list[None, :]).astype(jnp.bfloat16)
@@ -92,7 +106,7 @@
 
 
 def gather_columns(column_part):
-    return lax.all_gather(column_part, "tensor", axis=1, tiled=True)
+    return update_the_axis_part(column_part)
 
 
 def gather_gram(gram_part):

time: 154 us -> 150 us (0.974)
  between operations: 15.7 us -> 2.33 us
  starting transfers between devices: 40.2 us -> 45.5 us
  local copies, waits for them, and re-layouts: 13.7 us -> 17.8 us
    all_to_all x0 -> x1, waiting for transfers between devices: none -> 17.9 us  [map_floor_over_axis(): piece_now = lax.all_to_all(block_now, a_name, 0, 0)]
    all_gather x1 -> x0, waiting for transfers between devices: 16.5 us -> none  [gather_columns(): return lax.all_gather(column_part, 'tensor', axis=1, tiled=True)]
    all_to_all x0 -> x1, starting transfers between devices: none -> 4.14 us  [map_floor_over_axis(): piece_now = lax.all_to_all(block_now, a_name, 0, 0)]
    unnamed x25 -> x27, local copies, waits for them, and re-layouts: 7.42 us -> 10 us
    all_to_all x1, starting transfers between devices: 7.25 us -> 9.19 us  [per_device(): lax.all_to_all(vec_pieces, 'shard', split_axis=0, concat_axis=0, tiled=True)]
    reduce_sum x1, other arithmetic: 3.3 us -> 1.61 us  [normalized(): squares = jnp.sum(values * values)]
  transfers between devices with their start and end apart: 4 -> 4, of which waited for: 3 -> 3; matrix products, arithmetic and copies ran while one was open for 17% -> 16% of each run, Pallas kernels for 0% -> 0%
where the time goes in v1:
time: 150 us; the launch traced here: 149 us
  waiting for transfers between devices  55.2 us (37%)
  starting transfers between devices  45.5 us (30%)
  local copies, waits for them, and re-layouts  17.8 us (12%)
  matrix products  17.3 us (12%)
  other arithmetic  10.8 us (7%)
  between operations  2.33 us (2%)
    all_to_all x1, waiting for transfers between devices, per_device(): lax.all_to_all(route_rows(joint_map, joint_pieces), 'shard', split_axis=0...  18.8 us
    all_to_all x1, waiting for transfers between devices, per_device(): lax.all_to_all(own_result.reshape(shards, rows_dev, block_width), 'shard'...  18.6 us
    all_to_all x1, starting transfers between devices, per_device(): lax.all_to_all(route_rows(joint_map, joint_pieces), 'shard', split_axis=0...  18.4 us
    all_to_all x1, waiting for transfers between devices, map_floor_over_axis(): piece_now = lax.all_to_all(block_now, a_name, 0, 0)  17.9 us
    all_to_all x1, starting transfers between devices, per_device(): lax.all_to_all(own_result.reshape(shards, rows_dev, block_width), 'shard'...  13.7 us
    dot_general x4, matrix products, newton_step(): lax.dot_general(full_iterate, polynomial, (((1,), (1,)), ((), ())), prefe...  10.6 us
    unnamed x27, local copies, waits for them, and re-layouts  10 us
    all_to_all x1, starting transfers between devices, per_device(): lax.all_to_all(vec_pieces, 'shard', split_axis=0, concat_axis=0, tiled=True)  9.19 us
  transfers between devices with their start and end apart: 4, of which 3 were waited for; matrix products, arithmetic and copies ran while one was open for 16% of the time, Pallas kernels for 0%

profile of v1, /device:TPU:1, one launch (start us, length us, event | category | flops | bytes accessed | tf_op | source)
XLA Modules:
  0.0 149.0 jit_solution(17222949145101005453)
XLA Ops:
  0.6 0.8 slice_bitcast_fusion.1
  1.4 1.0 pad_maximum_fusion
  2.4 0.2 copy.32
  2.6 0.4 reshape.55
  3.0 0.1 pad_add_fusion
  3.1 0.3 convolution_convert_fusion
  3.4 0.3 copy.33
  3.7 0.0 copy-start.5
  3.7 1.4 copy.34
  5.1 1.6 %reshape.69 = bf16[128,2,960]{2,1,0:T(2,128)(2,1)} reshape(bf16[128,10,192]{2,1,0:T(8,128)(2,1)S(1)} %copy.34) | data formatting | bytes 983040
  6.6 18.4 %all-to-all-start = ((bf16[128,2,960]{2,1,0:T(2,128)(2,1)}), bf16[128,2,960]{2,1,0:T(2,128)(2,1)S(1)}, u32[]{:S(2)}, u32[]{:S(2)}) async-start(bf16[128,2,960]{2,1,0:T(2,128)(2,1)} %reshape.69), calls=%async_computation | async-start | bytes 1048576 | tf_op jit(solution)/shard_map/all_to_all | solution.py:137
  25.1 0.0 copy-done.5
  25.1 0.6 compare_reduce_fusion.1
  25.7 18.8 %all-to-all-done = bf16[128,2,960]{2,1,0:T(2,128)(2,1)S(1)} async-done(((bf16[128,2,960]{2,1,0:T(2,128)(2,1)}), bf16[128,2,960]{2,1,0:T(2,128)(2,1)S(1)}, u32[]{:S(2)}, u32[]{:S(2)}) %all-to-all-start) | async-done | bytes 491552 | tf_op jit(solution)/shard_map/all_to_all | solution.py:137
  44.5 0.8 reshape.70
  45.2 0.4 reshape.59
  45.6 0.0 copy-start.1
  45.6 0.4 copy.35
  46.0 0.8 copy-done.1
  46.8 4.8 %fusion.17 = (f32[1,192,1280]{2,1,0:T(8,128)}, bf16[1280,192]{0,1:T(8,128)(2,1)S(1)}, f32[1,192,1280]{2,1,0:T(8,128)}, f32[]{:T(128)}, bf16[192,1280]{1,0:T(8,128)(2,1)S(1)}) fusion(f32[1,192,1280]{2,1,0:T(8,128)S(1)} %copy-done.1, f32[1280,192]{0,1:T(8,128)S(1)} %copy.35, pred[]{:T(512)} %get-tuple-element.21, f32[1,192,1280]{2,1,0:T(8,128)} %param.16, ...), kind=kLoop, calls=%fused_computation.39 | loop fusion | flops 4177919 | bytes 5898246 | tf_op jit(solution)/shard_map/broadcast_in_dim | solution.py:175
  51.7 1.4 stack.2
  53.1 4.1 %all-to-all-start.1 = ((bf16[4,1280,192]{1,2,0:T(8,128)(2,1)}), bf16[4,1280,192]{1,2,0:T(8,128)(2,1)S(1)}, u32[]{:S(2)}, u32[]{:S(2)}) async-start(bf16[4,1280,192]{1,2,0:T(8,128)(2,1)} %stack.2), calls=%async_computation.1 | async-start | bytes 3932160 | tf_op jit(solution)/shard_map/all_to_all | solution.py:30
  57.2 0.5 broadcast.81
  57.7 1.0 reduce.7
  58.8 1.0 all_to_all.24
  60.5 0.3 convolution_convert_fusion.5
  60.8 0.4 fusion.3
  61.3 0.3 convolution_convert_fusion.4
  61.6 0.4 fusion.4
  62.0 17.9 %all-to-all-done.1 = bf16[4,1280,192]{1,2,0:T(8,128)(2,1)S(1)} async-done(((bf16[4,1280,192]{1,2,0:T(8,128)(2,1)}), bf16[4,1280,192]{1,2,0:T(8,128)(2,1)S(1)}, u32[]{:S(2)}, u32[]{:S(2)}) %all-to-all-start.1) | async-done | bytes 1966112 | tf_op jit(solution)/shard_map/all_to_all | solution.py:30
  79.9 9.2 %all-to-all-start.3 = ((f32[128,1,336]{2,1,0:T(1,128)}), f32[128,1,336]{2,1,0:T(1,128)S(1)}, u32[]{:S(2)}, u32[]{:S(2)}) async-start(f32[128,1,336]{2,1,0:T(1,128)} %all_to_all.24), calls=%async_computation.3 | async-start | bytes 393216 | tf_op jit(solution)/shard_map/all_to_all | solution.py:166
  89.1 1.6 %fusion = f32[]{:T(128)} fusion(bf16[4,1280,192]{1,2,0:T(8,128)(2,1)S(1)} %all-to-all-done.1), kind=kLoop, calls=%fused_computation.2 | loop fusion | flops 2949119 | bytes 1966084 | tf_op jit(solution)/shard_map/reduce_sum | solution.py:67
  91.4 0.4 fusion.1
  91.8 1.3 copy-done
  93.1 2.8 %convolution_convert_fusion.3 = bf16[768,768]{1,0:T(8,128)(2,1)} fusion(bf16[1280,768]{0,1:T(8,128)(2,1)S(1)} %bitcast.89), kind=kOutput, calls=%fused_computation.16 | convolution fusion | flops 1510539264 | bytes 3145728 | tf_op jit(solution)/shard_map/dot_general | solution.py:72
  95.8 6.0 %add_convert_fusion = bf16[1280,768]{0,1:T(8,128)(2,1)S(1)} fusion(bf16[1280,768]{0,1:T(8,128)(2,1)} %bitcast.90, bf16[768,768]{1,0:T(8,128)(2,1)} %convolution_convert_fusion.3), kind=kOutput, calls=%fused_computation.4 | convolution fusion | flops 2422800384 | bytes 5111808 | tf_op jit(solution)/shard_map/dot_general | solution.py:86
  101.8 1.3 copy-done.9
  103.1 2.8 %convolution_convert_fusion.2 = bf16[768,768]{1,0:T(8,128)(2,1)} fusion(bf16[1280,768]{0,1:T(8,128)(2,1)S(1)} %add_convert_fusion), kind=kOutput, calls=%fused_computation.15 | convolution fusion | flops 1510539264 | bytes 3145728 | tf_op jit(solution)/shard_map/dot_general | solution.py:72
  105.9 3.7 %fusion.5 = bf16[1280,192]{0,1:T(8,128)(2,1)S(1)} fusion(bf16[1280,192]{0,1:T(8,128)(2,1)S(1)} %fusion.4, bf16[1280,768]{0,1:T(8,128)(2,1)} %copy-done.9, bf16[768,768]{1,0:T(8,128)(2,1)} %convolution_convert_fusion.2, s32[]{:T(128)S(6)} %select_n.39, pred[]{:T(512)} %get-tuple-element.21), kind=kOutput, calls=%fused_computation.11 | convolution fusion | flops 605945856 | bytes 5212160 | tf_op jit(solution)/shard_map/dot_general | solution.py:86
  109.6 0.2 copy.36
  109.9 0.0 copy-start.6
  109.9 0.0 copy-start.7
  109.9 0.0 copy-start.8
  109.9 0.3 reshape.57
  110.2 1.6 %reshape.71 = bf16[128,2,960]{2,1,0:T(2,128)(2,1)} reshape(bf16[128,10,192]{2,1,0:T(8,128)(2,1)S(1)} %reshape.57) | data formatting | bytes 983040
  111.7 0.0 all-to-all-done.3
  111.7 13.7 %all-to-all-start.2 = ((bf16[128,2,960]{2,1,0:T(2,128)(2,1)}), bf16[128,2,960]{2,1,0:T(2,128)(2,1)S(1)}, u32[]{:S(2)}, u32[]{:S(2)}) async-start(bf16[128,2,960]{2,1,0:T(2,128)(2,1)} %reshape.71), calls=%async_computation.2 | async-start | bytes 1048576 | tf_op jit(solution)/shard_map/all_to_all | solution.py:154
  125.5 0.2 reduce_sum.29
  125.6 0.0 copy-done.6
  125.7 0.0 copy-done.8
  125.7 0.6 divide_subtract_fusion
  126.3 18.6 %all-to-all-done.2 = bf16[128,2,960]{2,1,0:T(2,128)(2,1)S(1)} async-done(((bf16[128,2,960]{2,1,0:T(2,128)(2,1)}), bf16[128,2,960]{2,1,0:T(2,128)(2,1)S(1)}, u32[]{:S(2)}, u32[]{:S(2)}) %all-to-all-start.2) | async-done | bytes 491552 | tf_op jit(solution)/shard_map/all_to_all | solution.py:154
  144.9 0.8 reshape.72
  145.6 0.0 copy-start.3
  145.7 0.7 copy.37
  146.4 0.3 convolution_convert_fusion.1
  146.7 0.0 copy-start.4
  146.8 0.2 mul.158
  147.0 0.0 copy-done.3
  147.0 0.2 fusion.26
  147.2 0.7 copy.40
  147.9 0.2 mul.162
  148.1 0.2 fusion.29
  148.2 0.7 copy.41
  (7 shorter events, 0.1 us)
Async XLA Ops:
  3.7 21.4 %copy-start.5 = (s32[2,32]{1,0:T(2,128)S(1)}, s32[2,32]{1,0:T(2,128)}, u32[]{:S(2)}) copy-start(s32[2,32]{1,0:T(2,128)} %param.17) | copy-start | bytes 772
  6.6 37.8 %all-to-all-start = ((bf16[128,2,960]{2,1,0:T(2,128)(2,1)}), bf16[128,2,960]{2,1,0:T(2,128)(2,1)S(1)}, u32[]{:S(2)}, u32[]{:S(2)}) async-start(bf16[128,2,960]{2,1,0:T(2,128)(2,1)} %reshape.69), calls=%async_computation | async-start | bytes 1048576 | tf_op jit(solution)/shard_map/all_to_all | solution.py:137
  45.6 1.2 copy-start.1
  53.1 4.7 %copy-start.2 = (f32[1,43008]{1,0:T(1,128)S(1)}, f32[1,43008]{1,0:T(1,128)}, u32[]{:S(2)}) copy-start(f32[1,43008]{1,0:T(1,128)} %param.18) | copy-start | bytes 516100
  53.1 26.8 %all-to-all-start.1 = ((bf16[4,1280,192]{1,2,0:T(8,128)(2,1)}), bf16[4,1280,192]{1,2,0:T(8,128)(2,1)S(1)}, u32[]{:S(2)}, u32[]{:S(2)}) async-start(bf16[4,1280,192]{1,2,0:T(8,128)(2,1)} %stack.2), calls=%async_computation.1 | async-start | bytes 3932160 | tf_op jit(solution)/shard_map/all_to_all | solution.py:30
  79.9 31.8 %all-to-all-start.3 = ((f32[128,1,336]{2,1,0:T(1,128)}), f32[128,1,336]{2,1,0:T(1,128)S(1)}, u32[]{:S(2)}, u32[]{:S(2)}) async-start(f32[128,1,336]{2,1,0:T(1,128)} %all_to_all.24), calls=%async_computation.3 | async-start | bytes 393216 | tf_op jit(solution)/shard_map/all_to_all | solution.py:166
  91.8 1.3 copy-start
  101.8 1.3 copy-start.9
  109.9 15.8 %copy-start.6 = (f32[336]{0:T(512)S(1)}, f32[336]{0:T(512)}, u32[]{:S(2)}) copy-start(f32[336]{0:T(512)} %param.19) | copy-start | bytes 4036
  109.9 15.8 %copy-start.7 = (f32[336]{0:T(512)S(1)}, f32[336]{0:T(512)}, u32[]{:S(2)}) copy-start(f32[336]{0:T(512)} %param.20) | copy-start | bytes 4036
  109.9 15.8 %copy-start.8 = (f32[336]{0:T(512)S(1)}, f32[336]{0:T(512)}, u32[]{:S(2)}) copy-start(f32[336]{0:T(512)} %param.21) | copy-start | bytes 4036
  111.7 33.2 %all-to-all-start.2 = ((bf16[128,2,960]{2,1,0:T(2,128)(2,1)}), bf16[128,2,960]{2,1,0:T(2,128)(2,1)S(1)}, u32[]{:S(2)}, u32[]{:S(2)}) async-start(bf16[128,2,960]{2,1,0:T(2,128)(2,1)} %reshape.71), calls=%async_computation.2 | async-start | bytes 1048576 | tf_op jit(solution)/shard_map/all_to_all | solution.py:154
  145.6 1.3 copy-start.3
  146.7 1.3 copy-start.4
